TPU v7x, 256 devices: a whole 4x4x8 slice. The times are simulated.
256 devices in a mesh: req: 32 (over x, z), mlp: 8 (over y, core).
Axes of the slice: x: 4, y: 4, z: 8, core: 2. Of those that a mesh axis runs over, the one named last changes fastest.
Arguments:
- x_pages: bfloat16 [1024, 8, 4096], P('req', None, 'mlp'), may hold values from -6 to 6
- page_owner: int32 [1024], P('req'), may hold values from 0 to 31, as said below
- request_id: int32 [8192], P('req'), may hold values from 0 to 8191, as said below
- adapter_table: int32 [8192], P('req'), may hold values from 0 to 63
- ln_gain: float32 [4096], replicated, may hold values from 0.5 to 1.5
- ln_bias: float32 [4096], replicated, may hold values from -3 to 3
- w_query: bfloat16 [4096, 2048], P('req', 'mlp'), may hold values from -0.09375 to 0.09375
- w_key: bfloat16 [4096, 2048], P('req', 'mlp'), may hold values from -0.09375 to 0.09375
- w_value: bfloat16 [4096, 2048], P('req', 'mlp'), may hold values from -0.09375 to 0.09375
- w_attn_out: bfloat16 [2048, 4096], P('mlp', 'req'), may hold values from -0.125 to 0.125
- down_query: bfloat16 [4096, 1024], P('mlp'), may hold values from -0.09375 to 0.09375
- up_query: bfloat16 [1024, 2048], P(None, 'mlp'), may hold values from -1.5 to 1.5
- down_value: bfloat16 [4096, 1024], P('mlp'), may hold values from -0.09375 to 0.09375
- up_value: bfloat16 [1024, 2048], P(None, 'mlp'), may hold values from -1.5 to 1.5
- w_fc_in: bfloat16 [4096, 8192], P('req', 'mlp'), may hold values from -0.09375 to 0.09375
- b_fc_in: float32 [8192], P('mlp'), may hold values from -3 to 3
- down_fc: bfloat16 [4096, 1024], P('mlp'), may hold values from -0.09375 to 0.09375
- up_fc: bfloat16 [1024, 8192], P(None, 'mlp'), may hold values from -1.5 to 1.5
- w_fc_out: bfloat16 [8192, 4096], P('mlp', 'req'), may hold values from -0.0625 to 0.0625
- b_fc_out: float32 [4096], P('mlp'), may hold values from -3 to 3
Outputs:
- out_pages: bfloat16 [1024, 8, 4096], P('req', None, 'mlp')
Inputs may be any that keep to these rules, and one draw needn't show every extreme that they name: `page_owner`: every owner receives exactly 32 pages, at most 2 of them from one device, and some device sends exactly 2 pages to some owner. `request_id`: ids never fall; every request lies inside one owner's block of 256 rows, and the ids of block k lie in k * 256 to k * 256 + 255; some request is 256 long.
All inputs are finite; a program needn't handle non-finite values.
Results may differ from a plain program's by a relative error of at most 0.006.
Values may be sent and summed in bfloat16 or wider, within the bound.
No kernel may reach another device: no remote copies, remote signals or barrier semaphores. Data moves between devices by JAX's collectives and lax.ppermute only.
A program may use at most 128 MiB of HBM per device.

v0:
```python
import jax
import jax.numpy as jnp
from jax import lax
from jax.sharding import PartitionSpec as P

HS = 256
ROT = 64
NAD = 64
R = 16
EPS = 1e-05


def gelu_tanh(v):
    return 0.5 * v * (1.0 + jnp.tanh(0.7978845608028654 * (v + 0.044715 * v * v * v)))


def rotate(block, pos):
    half = ROT // 2
    freq = jnp.power(10000.0, -jnp.arange(half).astype(jnp.float32) * 2.0 / ROT)
    angle = pos.astype(jnp.float32)[:, None, None] * freq[None, None, :]
    cosine = jnp.cos(angle)
    sine = jnp.sin(angle)
    even = block[:, :, 0:ROT:2]
    odd = block[:, :, 1:ROT:2]
    turned = jnp.stack([even * cosine - odd * sine, odd * cosine + even * sine], axis=-1)
    turned = turned.reshape(block.shape[0], block.shape[1], ROT)
    return jnp.concatenate([turned, block[:, :, ROT:]], axis=2)


def on_device(
    x_pages,
    page_owner,
    request_id,
    adapter_table,
    ln_gain,
    ln_bias,
    w_query,
    w_key,
    w_value,
    w_attn_out,
    down_query,
    up_query,
    down_value,
    up_value,
    w_fc_in,
    b_fc_in,
    down_fc,
    up_fc,
    w_fc_out,
    b_fc_out,
):
    groups = lax.axis_size("req")
    pg_dev = x_pages.shape[0]
    page_len = x_pages.shape[1]
    width_m = x_pages.shape[2]
    tok = request_id.shape[0]
    per_owner = pg_dev // groups + 1
    slots = groups * per_owner
    page_iota = jnp.arange(pg_dev)
    earlier = (page_owner[None, :] == page_owner[:, None]) & (
        page_iota[None, :] < page_iota[:, None]
    )
    rank = jnp.sum(earlier.astype(jnp.int32), axis=1)
    slot = page_owner * per_owner + rank
    place = (slot[None, :] == jnp.arange(slots)[:, None]).astype(jnp.bfloat16)
    flat_pages = x_pages.reshape(pg_dev, page_len * width_m)
    outgoing = jnp.dot(place, flat_pages, preferred_element_type=jnp.float32).astype(jnp.bfloat16)
    outgoing = outgoing.reshape(groups, per_owner, page_len * width_m)
    filled = jnp.sum(place, axis=1).reshape(groups, per_owner)
    arrived, marks = (
        lax.all_to_all(outgoing, "req", split_axis=0, concat_axis=0, tiled=True),
        lax.all_to_all(filled, "req", split_axis=0, concat_axis=0, tiled=True),
    )
    valid = marks.reshape(slots).astype(jnp.float32)
    position = jnp.cumsum(valid) - 1.0
    take = (
        (position[None, :] == jnp.arange(pg_dev).astype(jnp.float32)[:, None])
        & (valid[None, :] > 0.5)
    ).astype(jnp.bfloat16)
    own_x = jnp.dot(
        take, arrived.reshape(slots, page_len * width_m), preferred_element_type=jnp.float32
    )
    own_x = own_x.astype(jnp.bfloat16).reshape(tok, width_m)
    column = lax.axis_index("mlp") * width_m
    n_mlp = lax.axis_size("mlp")
    copies = jnp.broadcast_to(own_x[None], (n_mlp, tok, width_m))
    spread_x = lax.all_to_all(copies, "mlp", split_axis=0, concat_axis=0, tiled=True)
    whole = jnp.transpose(spread_x, (1, 0, 2)).reshape(tok, n_mlp * width_m).astype(jnp.float32)
    mean = jnp.mean(whole, axis=1, keepdims=True)
    var = jnp.mean(jnp.square(whole - mean), axis=1, keepdims=True)
    full_ln = ((whole - mean) * lax.rsqrt(var + EPS) * ln_gain + ln_bias).astype(jnp.bfloat16)
    ln_m = lax.dynamic_slice_in_dim(full_ln, column, width_m, 1)
    local_req = request_id - lax.axis_index("req") * tok
    lookup = local_req[:, None] == jnp.arange(tok)[None, :]
    adapter = jnp.sum(jnp.where(lookup, adapter_table[None, :], 0), axis=1)
    onehot = (adapter[:, None] == jnp.arange(NAD)[None, :]).astype(jnp.float32)
    onehot_low = onehot.astype(jnp.bfloat16)

    def pick(down):
        spread = jnp.dot(ln_m, down, preferred_element_type=jnp.float32).reshape(tok, NAD, R)
        return jnp.sum(spread * onehot[:, :, None], axis=1)

    picked = lax.psum((pick(down_query), pick(down_value), pick(down_fc)), "mlp")

    def lift(chosen, up):
        expanded = (onehot_low[:, :, None] * chosen.astype(jnp.bfloat16)[:, None, :]).reshape(
            tok, NAD * R
        )
        return jnp.dot(expanded, up, preferred_element_type=jnp.float32)

    row_iota = jnp.arange(tok)
    start = jnp.sum((request_id[None, :] < request_id[:, None]).astype(jnp.int32), axis=1)
    pos = row_iota - start
    mask = (request_id[:, None] == request_id[None, :]) & (row_iota[None, :] <= row_iota[:, None])
    heads_w = w_query.shape[1]
    ff_w = w_fc_in.shape[1]
    packed = jnp.concatenate([w_query, w_key, w_value, w_fc_in, w_attn_out.T], axis=1)
    fo_copies = jnp.broadcast_to(w_fc_out[None], (groups,) + w_fc_out.shape)
    fo_rows = lax.all_to_all(fo_copies, "req", split_axis=0, concat_axis=0, tiled=True)
    gathered = lax.all_gather(packed, "req", axis=0, tiled=True)
    n_in = 3 * heads_w + ff_w
    base = jnp.dot(full_ln, gathered[:, :n_in], preferred_element_type=jnp.float32)
    base_q = base[:, :heads_w]
    base_k = base[:, heads_w : 2 * heads_w]
    base_v = base[:, 2 * heads_w : 3 * heads_w]
    query = rotate(
        (base_q + lift(picked[0], up_query)).reshape(tok, heads_w // HS, HS), pos
    ).astype(jnp.bfloat16)
    keys = rotate(base_k.reshape(tok, heads_w // HS, HS), pos).astype(jnp.bfloat16)
    value = (
        (base_v + lift(picked[1], up_value)).astype(jnp.bfloat16).reshape(tok, heads_w // HS, HS)
    )
    scores = jnp.einsum("qhd,khd->hqk", query, keys, preferred_element_type=jnp.float32) * HS ** (
        -0.5
    )
    scores = jnp.where(mask[None, :, :], scores, -1e30)
    top = jnp.max(scores, axis=2, keepdims=True)
    weights = jnp.exp(scores - top)
    probs = (weights / jnp.sum(weights, axis=2, keepdims=True)).astype(jnp.bfloat16)
    mixed_heads = jnp.einsum("hqk,khd->qhd", probs, value, preferred_element_type=jnp.float32)
    attn = mixed_heads.astype(jnp.bfloat16).reshape(tok, heads_w)
    hidden_pre = base[:, 3 * heads_w :]
    hidden_pre = hidden_pre + lift(picked[2], up_fc) + b_fc_in
    hidden = gelu_tanh(hidden_pre).astype(jnp.bfloat16)
    part = lax.dot_general(
        attn, gathered[:, n_in:], (((1,), (1,)), ((), ())), preferred_element_type=jnp.float32
    )
    part = part + jnp.einsum(
        "tf,rfc->trc", hidden, fo_rows, preferred_element_type=jnp.float32
    ).reshape(tok, groups * fo_rows.shape[2])
    shares = lax.psum_scatter(part, "mlp", scatter_dimension=1, tiled=True)
    result = (own_x.astype(jnp.float32) + shares + b_fc_out).astype(jnp.bfloat16)
    back_flat = result.reshape(pg_dev, page_len * width_m)
    leaving = jnp.dot(take.T, back_flat, preferred_element_type=jnp.float32).astype(jnp.bfloat16)
    leaving = leaving.reshape(groups, per_owner, page_len * width_m)
    returned = lax.all_to_all(leaving, "req", split_axis=0, concat_axis=0, tiled=True)
    pages_back = jnp.dot(
        place.T, returned.reshape(slots, page_len * width_m), preferred_element_type=jnp.float32
    )
    return pages_back.astype(jnp.bfloat16).reshape(pg_dev, page_len, width_m)


def solution(mesh):
    in_specs = (
        P("req", None, "mlp"),
        P("req"),
        P("req"),
        P("req"),
        P(),
        P(),
        P("req", "mlp"),
        P("req", "mlp"),
        P("req", "mlp"),
        P("mlp", "req"),
        P("mlp", None),
        P(None, "mlp"),
        P("mlp", None),
        P(None, "mlp"),
        P("req", "mlp"),
        P("mlp"),
        P("mlp", None),
        P(None, "mlp"),
        P("mlp", "req"),
        P("mlp"),
    )
    out_specs = P("req", None, "mlp")
    return jax.shard_map(
        on_device, mesh=mesh, in_specs=in_specs, out_specs=out_specs, check_vma=False
    )
```

profile of v0, /device:TPU:57, one launch (start us, length us, event | category | flops | bytes accessed | tf_op | source)
XLA Modules:
  0.0 442.5 jit_solution(15995266762931642183)
XLA Ops:
  14.4 10.6 %all-to-all-start = ((bf16[32,1,2]{2,1,0:T(2,128)(2,1)}), bf16[32,1,2]{2,1,0:T(2,128)(2,1)S(1)}, u32[]{:S(2)}, u32[]{:S(2)}) async-start(bf16[32,1,2]{2,1,0:T(2,128)(2,1)} %all_to_all.24), calls=%async_computation | async-start | bytes 32768 | tf_op jit(solution)/shard_map/all_to_all | solution.py:72
  27.6 5.2 %all-to-all-done = bf16[32,1,2]{2,1,0:T(2,128)(2,1)S(1)} async-done(((bf16[32,1,2]{2,1,0:T(2,128)(2,1)}), bf16[32,1,2]{2,1,0:T(2,128)(2,1)S(1)}, u32[]{:S(2)}, u32[]{:S(2)}) %all-to-all-start) | async-done | bytes 160 | tf_op jit(solution)/shard_map/all_to_all | solution.py:72
  32.8 4.6 %all-to-all-start.1 = ((bf16[32,2,4096]{2,1,0:T(2,128)(2,1)}), bf16[32,2,4096]{2,1,0:T(2,128)(2,1)S(1)}, u32[]{:S(2)}, u32[]{:S(2)}) async-start(bf16[32,2,4096]{2,1,0:T(2,128)(2,1)} %reshape.352), calls=%async_computation.1 | async-start | bytes 1048576 | tf_op jit(solution)/shard_map/all_to_all | solution.py:71
  38.0 21.4 %all-to-all-done.1 = bf16[32,2,4096]{2,1,0:T(2,128)(2,1)S(1)} async-done(((bf16[32,2,4096]{2,1,0:T(2,128)(2,1)}), bf16[32,2,4096]{2,1,0:T(2,128)(2,1)S(1)}, u32[]{:S(2)}, u32[]{:S(2)}) %all-to-all-start.1) | async-done | bytes 524320 | tf_op jit(solution)/shard_map/all_to_all | solution.py:71
  61.7 7.6 %all-to-all-start.2 = ((bf16[8,256,512]{1,2,0:T(8,128)(2,1)}), bf16[8,256,512]{1,2,0:T(8,128)(2,1)}, u32[]{:S(2)}, u32[]{:S(2)}) async-start(bf16[8,256,512]{1,2,0:T(8,128)(2,1)} %broadcast_in_dim.15), calls=%async_computation.2 | async-start | bytes 4194304 | tf_op jit(solution)/shard_map/all_to_all | solution.py:87
  69.4 24.5 %all-to-all-done.2 = bf16[8,256,512]{1,2,0:T(8,128)(2,1)} async-done(((bf16[8,256,512]{1,2,0:T(8,128)(2,1)}), bf16[8,256,512]{1,2,0:T(8,128)(2,1)}, u32[]{:S(2)}, u32[]{:S(2)}) %all-to-all-start.2) | async-done | bytes 2097184 | tf_op jit(solution)/shard_map/all_to_all | solution.py:87
  93.9 4.3 broadcast_in_dim.19
  98.2 4.9 %all-to-all-start.3 = ((bf16[32,1024,128]{1,2,0:T(8,128)(2,1)}), bf16[32,1024,128]{1,2,0:T(8,128)(2,1)}, u32[]{:S(2)}, u32[]{:S(2)}) async-start(bf16[32,1024,128]{1,2,0:T(8,128)(2,1)} %broadcast_in_dim.19), calls=%async_computation.3 | async-start | bytes 16777216 | tf_op jit(solution)/shard_map/all_to_all | solution.py:119
  104.6 2.3 convert_reduce_fusion
  106.9 2.3 multiply_reduce_fusion
  109.2 2.6 fusion.5
  114.0 25.8 %all-reduce = (bf16[256,16]{0,1:T(8,128)(2,1)S(1)}, bf16[256,16]{0,1:T(8,128)(2,1)S(1)}, bf16[256,16]{0,1:T(8,128)(2,1)S(1)}) all-reduce(f32[256,16]{0,1:T(8,128)S(1)} %get-tuple-element.6, f32[256,16]{0,1:T(8,128)S(1)} %get-tuple-element.7, f32[256,16]{0,1:T(8,128)S(1)} %get-tuple-element.5), channel_id=1, replica_groups=mesh['req'=32,'mlp'=8] {'mlp'}, use_global_device_ids=true, to_apply=%region_14.15 | all-reduce | flops 12288 | bytes 73728 | tf_op jit(solution)/shard_map/psum | solution.py:103
  140.7 166.7 %all-gather.2.cloned.1.call-done = bf16[4096,2048]{1,0:T(8,128)(2,1)} async-done(((bf16[128,2048]{1,0:T(8,128)(2,1)}), bf16[4096,2048]{1,0:T(8,128)(2,1)}) %all-gather.2.cloned.1.call-update) | async-done | bytes 16777232 | tf_op jit(solution)/shard_map/all_gather | solution.py:120
  307.3 8.6 %fusion = f32[256,1792]{1,0:T(8,128)S(1)} fusion(bf16[256,4096]{0,1:T(8,128)(2,1)} %copy-done.1, bf16[4096,2048]{1,0:T(8,128)(2,1)} %all-gather.2.cloned.1.call-done), kind=kOutput, calls=%fused_computation | convolution fusion | flops 3758096384 | bytes 18612224 | tf_op jit(solution)/shard_map/dot_general | solution.py:122
  317.8 2.1 slice.46
  319.9 2.6 slice.45
  322.6 2.2 fusion.9
  324.7 2.1 slice.41
  326.8 2.1 slice.42
  334.2 12.2 %all-to-all-done.3 = bf16[32,1024,128]{1,2,0:T(8,128)(2,1)} async-done(((bf16[32,1024,128]{1,2,0:T(8,128)(2,1)}), bf16[32,1024,128]{1,2,0:T(8,128)(2,1)}, u32[]{:S(2)}, u32[]{:S(2)}) %all-to-all-start.3) | async-done | bytes 8388640 | tf_op jit(solution)/shard_map/all_to_all | solution.py:119
  346.4 8.9 %fusion.17 = f32[256,4096]{1,0:T(8,128)} fusion(bf16[1024,4096]{0,1:T(8,128)(2,1)} %bitcast.21, bf16[256,1024]{0,1:T(8,128)(2,1)S(1)} %bitcast.77, bf16[1024,1024]{1,0:T(8,128)(2,1)S(1)} %copy-done, f32[256,1792]{1,0:T(8,128)} %copy-done.2, f32[1024]{0:T(1024)S(1)} %copy-done.10), kind=kOutput, calls=%fused_computation.34 | convolution fusion | flops 2687238144 | bytes 16257024 | tf_op jit(solution)/shard_map/reshape | solution.py:150
  355.3 5.8 %convolution_add_fusion = f32[256,4096]{1,0:T(8,128)} fusion(f32[256,4096]{1,0:T(8,128)} %fusion.17, bf16[4096,2048]{1,0:T(8,128)(2,1)} %all-gather.2.cloned.1.call-done, bf16[256,256]{1,0:T(8,128)(2,1)S(1)} %fusion.10, f32[256,256]{0,1:T(8,128)S(1)} %get-tuple-element.23, f32[256]{0:T(256)S(1)} %fusion.24, f32[256]{0:T(256)S(1)} %get-tuple-element.22), kind=kOutput, calls=%fused_computation.2 | convolution fusion | flops 571736064 | bytes 10881024 | tf_op jit(solution)/shard_map/dot_general | solution.py:145
  361.1 43.3 %reduce-scatter.2.cloned.1.call-done = f32[256,512]{1,0:T(8,128)} async-done(((f32[256,4096]{1,0:T(8,128)}), f32[256,512]{1,0:T(8,128)}) %reduce-scatter.2.cloned.1.call-update) | async-done | bytes 524304 | tf_op jit(solution)/shard_map/reduce_scatter | solution.py:151
  406.4 26.9 %all_to_all.30 = bf16[32,2,4096]{2,1,0:T(2,128)(2,1)} all-to-all(bf16[32,2,4096]{2,1,0:T(2,128)(2,1)S(1)} %reshape.363), channel_id=1, replica_groups=mesh['req'=32,'mlp'=8] {'req'}, dimensions={0} | all-to-all | bytes 1048576 | tf_op jit(solution)/shard_map/all_to_all | solution.py:156
  (99 shorter events, 29.3 us)
Async XLA Ops:
  6.5 339.8 %copy-start = (bf16[1024,1024]{1,0:T(8,128)(2,1)S(1)}, bf16[1024,1024]{1,0:T(8,128)(2,1)}, u32[]{:S(2)}) copy-start(bf16[1024,1024]{1,0:T(8,128)(2,1)} %param.37) | copy-start | bytes 6291460
  6.5 300.8 %all-gather.2.cloned.1.call-start = ((), (), s32[]{:S(2)}) async-start(), calls=%async_computation.6 | async-start | bytes 17301504 | tf_op jit(solution)/shard_map/all_gather | solution.py:120
  11.2 0.8 copy-start.6
  13.6 23.9 %copy-start.13 = (s32[32]{0:T(128)}, s32[32]{0:T(128)S(1)}, u32[]{:S(2)}) copy-start(s32[32]{0:T(128)S(1)} %multiply_add_fusion.1) | copy-start | bytes 388
  14.4 18.4 %all-to-all-start = ((bf16[32,1,2]{2,1,0:T(2,128)(2,1)}), bf16[32,1,2]{2,1,0:T(2,128)(2,1)S(1)}, u32[]{:S(2)}, u32[]{:S(2)}) async-start(bf16[32,1,2]{2,1,0:T(2,128)(2,1)} %all_to_all.24), calls=%async_computation | async-start | bytes 32768 | tf_op jit(solution)/shard_map/all_to_all | solution.py:72
  32.8 26.6 %all-to-all-start.1 = ((bf16[32,2,4096]{2,1,0:T(2,128)(2,1)}), bf16[32,2,4096]{2,1,0:T(2,128)(2,1)S(1)}, u32[]{:S(2)}, u32[]{:S(2)}) async-start(bf16[32,2,4096]{2,1,0:T(2,128)(2,1)} %reshape.352), calls=%async_computation.1 | async-start | bytes 1048576 | tf_op jit(solution)/shard_map/all_to_all | solution.py:71
  37.4 24.2 %copy-start.15 = (f32[32]{0:T(128)}, f32[32]{0:T(128)S(1)}, u32[]{:S(2)}) copy-start(f32[32]{0:T(128)S(1)} %iota_convert_fusion) | copy-start | bytes 388
  59.6 9.6 %copy-start.7 = (bf16[1024,128]{1,0:T(8,128)(2,1)S(1)}, bf16[1024,128]{1,0:T(8,128)(2,1)}, u32[]{:S(2)}) copy-start(bf16[1024,128]{1,0:T(8,128)(2,1)} %param.38) | copy-start | bytes 786436
  61.7 32.2 %all-to-all-start.2 = ((bf16[8,256,512]{1,2,0:T(8,128)(2,1)}), bf16[8,256,512]{1,2,0:T(8,128)(2,1)}, u32[]{:S(2)}, u32[]{:S(2)}) async-start(bf16[8,256,512]{1,2,0:T(8,128)(2,1)} %broadcast_in_dim.15), calls=%async_computation.2 | async-start | bytes 4194304 | tf_op jit(solution)/shard_map/all_to_all | solution.py:87
  98.2 5.5 %copy-start.11 = (s32[256]{0:T(256)S(1)}, s32[256]{0:T(256)}, u32[]{:S(2)}) copy-start(s32[256]{0:T(256)} %param.22) | copy-start | bytes 3076
  98.2 5.6 %copy-start.17 = (s32[256]{0:T(256)S(1)}, s32[256]{0:T(256)}, u32[]{:S(2)}) copy-start(s32[256]{0:T(256)} %param.23) | copy-start | bytes 3076
  98.2 248.2 %all-to-all-start.3 = ((bf16[32,1024,128]{1,2,0:T(8,128)(2,1)}), bf16[32,1024,128]{1,2,0:T(8,128)(2,1)}, u32[]{:S(2)}, u32[]{:S(2)}) async-start(bf16[32,1024,128]{1,2,0:T(8,128)(2,1)} %broadcast_in_dim.19), calls=%async_computation.3 | async-start | bytes 16777216 | tf_op jit(solution)/shard_map/all_to_all | solution.py:119
  103.1 6.1 %copy-start.8 = (f32[4096]{0:T(1024)S(1)}, f32[4096]{0:T(1024)}, u32[]{:S(2)}) copy-start(f32[4096]{0:T(1024)} %param.25) | copy-start | bytes 49156
  103.1 6.1 %copy-start.9 = (f32[4096]{0:T(1024)S(1)}, f32[4096]{0:T(1024)}, u32[]{:S(2)}) copy-start(f32[4096]{0:T(1024)} %param.24) | copy-start | bytes 49156
  103.1 301.3 %reduce-scatter.2.cloned.1.call-start = ((), (), s32[]{:S(2)}) async-start(), calls=%async_computation.7 | async-start | bytes 4718592 | tf_op jit(solution)/shard_map/reduce_scatter | solution.py:151
  104.6 7.2 %copy-start.3 = (bf16[512,1024]{1,0:T(8,128)(2,1)S(1)}, bf16[512,1024]{1,0:T(8,128)(2,1)}, u32[]{:S(2)}) copy-start(bf16[512,1024]{1,0:T(8,128)(2,1)} %param.30) | copy-start | bytes 3145732
  106.9 5.5 %copy-start.4 = (bf16[512,1024]{1,0:T(8,128)(2,1)S(1)}, bf16[512,1024]{1,0:T(8,128)(2,1)}, u32[]{:S(2)}) copy-start(bf16[512,1024]{1,0:T(8,128)(2,1)} %param.36) | copy-start | bytes 3145732
  109.2 3.8 copy-start.5
  111.8 2.2 copy-start.1
  315.9 1.2 copy-start.2
  317.1 29.3 %copy-start.10 = (f32[1024]{0:T(1024)S(1)}, f32[1024]{0:T(1024)}, u32[]{:S(2)}) copy-start(f32[1024]{0:T(1024)} %param.35) | copy-start | bytes 12292
  361.1 43.3 %copy-start.12 = (f32[512]{0:T(512)S(1)}, f32[512]{0:T(512)}, u32[]{:S(2)}) copy-start(f32[512]{0:T(512)} %param.39) | copy-start | bytes 6148
  361.1 44.6 %copy-start.16 = (f32[32]{0:T(128)S(1)}, f32[32]{0:T(128)}, u32[]{:S(2)}) copy-start(f32[32]{0:T(128)} %copy-done.15) | copy-start | bytes 388
  361.1 73.5 %copy-start.14 = (s32[32]{0:T(128)S(1)}, s32[32]{0:T(128)}, u32[]{:S(2)}) copy-start(s32[32]{0:T(128)} %copy-done.13) | copy-start | bytes 388
Sparse Core Ops, SparseCore 0:
  12.1 295.1 all-gather.1
  361.2 43.1 reduce-scatter.1
where the time goes:
time: 443 us; the launch traced here: 442 us
  waiting for transfers between devices  273 us (62%)
  blocking collectives  52.7 us (12%)
  matrix products  30.4 us (7%)
  local copies, waits for them, and re-layouts  29.9 us (7%)
  starting transfers between devices  27.7 us (6%)
  other arithmetic  14.7 us (3%)
  between operations  13.9 us (3%)
    all_gather x1, waiting for transfers between devices, on_device(): gathered = lax.all_gather(packed, 'req', axis=0, tiled=True)  167 us
    reduce_scatter x1, waiting for transfers between devices, on_device(): shares = lax.psum_scatter(part, 'mlp', scatter_dimension=1, tiled=True)  43.3 us
    all_to_all x1, blocking collectives, on_device(): lax.all_to_all(leaving, 'req', split_axis=0, concat_axis=0, tiled=True)  26.9 us
    psum x1, blocking collectives, on_device(): lax.psum((pick(down_query), pick(down_value), pick(down_fc)), 'mlp')  25.8 us
    all_to_all x1, waiting for transfers between devices, on_device(): lax.all_to_all(copies, 'mlp', split_axis=0, concat_axis=0, tiled=True)  24.5 us
    all_to_all x1, waiting for transfers between devices, on_device(): lax.all_to_all(outgoing, 'req', split_axis=0, concat_axis=0, tiled=True)  21.4 us
    all_to_all x1, waiting for transfers between devices, on_device(): lax.all_to_all(fo_copies, 'req', split_axis=0, concat_axis=0, tiled=True)  12.2 us
    all_to_all x1, starting transfers between devices, on_device(): lax.all_to_all(filled, 'req', split_axis=0, concat_axis=0, tiled=True)  10.6 us
  transfers between devices with their start and end apart: 6, of which 6 were waited for; matrix products, arithmetic and copies ran while one was open for 11% of the time, Pallas kernels for 0%

commit v1 on v0

--- a/solution.py
+++ b/solution.py
@@ -1,13 +1,24 @@
+import functools
 import jax
 import jax.numpy as jnp
 from jax import lax
 from jax.sharding import PartitionSpec as P
+from jax.lax import all_to_all, axis_size
 
 HS = 256
 ROT = 64
 NAD = 64
 R = 16
 EPS = 1e-05
+
+
+def balance_positions_now(panel, across):
+    return jnp.concatenate(
+        all_to_all(jnp.stack([panel] * axis_size(across), axis=0), across, 0, 0), axis=0
+    )
+
+
+compute_sizes = functools.partial(balance_positions_now, across="req")
 
 
 def gelu_tanh(v):
@@ -117,7 +128,7 @@
     packed = jnp.concatenate([w_query, w_key, w_value, w_fc_in, w_attn_out.T], axis=1)
     fo_copies = jnp.broadcast_to(w_fc_out[None], (groups,) + w_fc_out.shape)
     fo_rows = lax.all_to_all(fo_copies, "req", split_axis=0, concat_axis=0, tiled=True)
-    gathered = lax.all_gather(packed, "req", axis=0, tiled=True)
+    gathered = compute_sizes(packed)
     n_in = 3 * heads_w + ff_w
     base = jnp.dot(full_ln, gathered[:, :n_in], preferred_element_type=jnp.float32)
     base_q = base[:, :heads_w]

time: 443 us -> 806 us (1.82)
  waiting for transfers between devices: 273 us -> 605 us
  starting transfers between devices: 27.7 us -> 45.7 us
  blocking collectives: 52.7 us -> 62 us
    all_to_all x0 -> x1, waiting for transfers between devices: none -> 386 us  [balance_positions_now(): all_to_all(jnp.stack([panel] * axis_size(across), axis=0), across, 0, 0)]
    all_gather x1 -> x0, waiting for transfers between devices: 167 us -> none  [on_device(): gathered = lax.all_gather(packed, 'req', axis=0, tiled=True)]
    all_to_all x1, waiting for transfers between devices: 12.2 us -> 114 us  [on_device(): lax.all_to_all(fo_copies, 'req', split_axis=0, concat_axis=0, tiled=True)]
    reduce_scatter x1, waiting for transfers between devices: 43.3 us -> 59.7 us  [on_device(): shares = lax.psum_scatter(part, 'mlp', scatter_dimension=1, tiled=True)]
    all_to_all x1, starting transfers between devices: 4.88 us -> 17.6 us  [on_device(): lax.all_to_all(fo_copies, 'req', split_axis=0, concat_axis=0, tiled=True)]
    psum x1, blocking collectives: 25.8 us -> 35 us  [on_device(): lax.psum((pick(down_query), pick(down_value), pick(down_fc)), 'mlp')]
  transfers between devices with their start and end apart: 6 -> 6, of which waited for: 6 -> 6; matrix products, arithmetic and copies ran while one was open for 11% -> 5% of each run, Pallas kernels for 0% -> 0%
where the time goes in v1:
time: 806 us; the launch traced here: 805 us
  waiting for transfers between devices  605 us (75%)
  blocking collectives  62 us (8%)
  starting transfers between devices  45.7 us (6%)
  local copies, waits for them, and re-layouts  33.3 us (4%)
  matrix products  29.5 us (4%)
  other arithmetic  15.5 us (2%)
  between operations  13.9 us (2%)
    all_to_all x1, waiting for transfers between devices, balance_positions_now(): all_to_all(jnp.stack([panel] * axis_size(across), axis=0), across, 0, 0)  386 us
    all_to_all x1, waiting for transfers between devices, on_device(): lax.all_to_all(fo_copies, 'req', split_axis=0, concat_axis=0, tiled=True)  114 us
    reduce_scatter x1, waiting for transfers between devices, on_device(): shares = lax.psum_scatter(part, 'mlp', scatter_dimension=1, tiled=True)  59.7 us
    psum x1, blocking collectives, on_device(): lax.psum((pick(down_query), pick(down_value), pick(down_fc)), 'mlp')  35 us
    all_to_all x1, blocking collectives, on_device(): lax.all_to_all(leaving, 'req', split_axis=0, concat_axis=0, tiled=True)  26.9 us
    all_to_all x1, waiting for transfers between devices, on_device(): lax.all_to_all(copies, 'mlp', split_axis=0, concat_axis=0, tiled=True)  24.4 us
    all_to_all x1, starting transfers between devices, on_device(): lax.all_to_all(fo_copies, 'req', split_axis=0, concat_axis=0, tiled=True)  17.6 us
  transfers between devices with their start and end apart: 6, of which 6 were waited for; matrix products, arithmetic and copies ran while one was open for 5% of the time, Pallas kernels for 0%

profile of v1, /device:TPU:57, one launch (start us, length us, event | category | flops | bytes accessed | tf_op | source)
XLA Modules:
  0.0 804.6 jit_solution(10880859803325053617)
XLA Ops:
  9.0 10.6 %all-to-all-start = ((bf16[32,1,2]{2,1,0:T(2,128)(2,1)}), bf16[32,1,2]{2,1,0:T(2,128)(2,1)S(1)}, u32[]{:S(2)}, u32[]{:S(2)}) async-start(bf16[32,1,2]{2,1,0:T(2,128)(2,1)} %all_to_all.28), calls=%async_computation | async-start | bytes 32768 | tf_op jit(solution)/shard_map/all_to_all | solution.py:83
  22.3 5.1 all-to-all-done
  27.4 4.7 all-to-all-start.1
  32.6 15.0 %all-to-all-done.1 = bf16[32,2,4096]{2,1,0:T(2,128)(2,1)S(1)} async-done(((bf16[32,2,4096]{2,1,0:T(2,128)(2,1)}), bf16[32,2,4096]{2,1,0:T(2,128)(2,1)S(1)}, u32[]{:S(2)}, u32[]{:S(2)}) %all-to-all-start.1) | async-done | bytes 524320 | tf_op jit(solution)/shard_map/all_to_all | solution.py:82
  49.9 7.7 all-to-all-start.2
  57.8 24.4 %all-to-all-done.2 = bf16[8,256,512]{1,2,0:T(8,128)(2,1)} async-done(((bf16[8,256,512]{1,2,0:T(8,128)(2,1)}), bf16[8,256,512]{1,2,0:T(8,128)(2,1)}, u32[]{:S(2)}, u32[]{:S(2)}) %all-to-all-start.2) | async-done | bytes 2097184 | tf_op jit(solution)/shard_map/all_to_all | solution.py:98
  82.2 5.9 stack.20
  88.2 5.1 all-to-all-start.3
  93.4 386.5 %all-to-all-done.3 = bf16[32,128,2048]{2,1,0:T(8,128)(2,1)} async-done(((bf16[32,128,2048]{2,1,0:T(8,128)(2,1)}), bf16[32,128,2048]{2,1,0:T(8,128)(2,1)}, u32[]{:S(2)}, u32[]{:S(2)}) %all-to-all-start.3) | async-done | bytes 16777248 | tf_op jit(solution)/shard_map/all_to_all | solution.py:17
  479.9 4.3 broadcast_in_dim.19
  484.2 17.6 %all-to-all-start.4 = ((bf16[32,1024,128]{1,2,0:T(8,128)(2,1)}), bf16[32,1024,128]{1,2,0:T(8,128)(2,1)}, u32[]{:S(2)}, u32[]{:S(2)}) async-start(bf16[32,1024,128]{1,2,0:T(8,128)(2,1)} %broadcast_in_dim.19), calls=%async_computation.4 | async-start | bytes 16777216 | tf_op jit(solution)/shard_map/all_to_all | solution.py:130
  503.4 2.2 convert_reduce_fusion
  505.6 2.3 multiply_reduce_fusion
  507.9 2.6 fusion.5
  512.7 35.0 %all-reduce = (bf16[256,16]{0,1:T(8,128)(2,1)S(1)}, bf16[256,16]{0,1:T(8,128)(2,1)S(1)}, bf16[256,16]{0,1:T(8,128)(2,1)S(1)}) all-reduce(f32[256,16]{0,1:T(8,128)S(1)} %get-tuple-element.6, f32[256,16]{0,1:T(8,128)S(1)} %get-tuple-element.7, f32[256,16]{0,1:T(8,128)S(1)} %get-tuple-element.5), channel_id=1, replica_groups=mesh['req'=32,'mlp'=8] {'mlp'}, use_global_device_ids=true, to_apply=%region_14.15 | all-reduce | flops 12288 | bytes 73728 | tf_op jit(solution)/shard_map/psum | solution.py:114
  548.7 8.6 %fusion = f32[256,1792]{1,0:T(8,128)S(1)} fusion(bf16[256,4096]{0,1:T(8,128)(2,1)} %copy-done.1, bf16[4096,2048]{1,0:T(8,128)(2,1)} %bitcast.3), kind=kOutput, calls=%fused_computation | convolution fusion | flops 3758096384 | bytes 18612224 | tf_op jit(solution)/shard_map/dot_general | solution.py:133
  560.1 1.9 slice.42
  562.9 1.8 slice.45
  564.8 1.9 slice.46
  578.1 113.9 %all-to-all-done.4 = bf16[32,1024,128]{1,2,0:T(8,128)(2,1)} async-done(((bf16[32,1024,128]{1,2,0:T(8,128)(2,1)}), bf16[32,1024,128]{1,2,0:T(8,128)(2,1)}, u32[]{:S(2)}, u32[]{:S(2)}) %all-to-all-start.4) | async-done | bytes 8388640 | tf_op jit(solution)/shard_map/all_to_all | solution.py:130
  692.0 8.9 %fusion.17 = f32[256,4096]{1,0:T(8,128)} fusion(bf16[1024,4096]{0,1:T(8,128)(2,1)} %bitcast.22, bf16[256,1024]{0,1:T(8,128)(2,1)S(1)} %bitcast.78, bf16[1024,1024]{1,0:T(8,128)(2,1)S(1)} %copy-done, f32[256,1792]{1,0:T(8,128)} %copy-done.2, f32[1024]{0:T(1024)S(1)} %copy-done.15), kind=kOutput, calls=%fused_computation.34 | convolution fusion | flops 2687238144 | bytes 16257024 | tf_op jit(solution)/shard_map/reshape | solution.py:161
  700.9 5.8 convolution_add_fusion
  706.7 59.7 %reduce-scatter.2.cloned.1.call-done = f32[256,512]{1,0:T(8,128)} async-done(((f32[256,4096]{1,0:T(8,128)}), f32[256,512]{1,0:T(8,128)}) %reduce-scatter.2.cloned.1.call-update) | async-done | bytes 524304 | tf_op jit(solution)/shard_map/reduce_scatter | solution.py:162
  768.5 26.9 %all_to_all.35 = bf16[32,2,4096]{2,1,0:T(2,128)(2,1)} all-to-all(bf16[32,2,4096]{2,1,0:T(2,128)(2,1)S(1)} %reshape.369), channel_id=1, replica_groups=mesh['req'=32,'mlp'=8] {'req'}, dimensions={0} | all-to-all | bytes 1048576 | tf_op jit(solution)/shard_map/all_to_all | solution.py:167
  (109 shorter events, 32.2 us)
Async XLA Ops:
  6.5 685.5 %copy-start = (bf16[1024,1024]{1,0:T(8,128)(2,1)S(1)}, bf16[1024,1024]{1,0:T(8,128)(2,1)}, u32[]{:S(2)}) copy-start(bf16[1024,1024]{1,0:T(8,128)(2,1)} %param.37) | copy-start | bytes 6291460
  8.2 23.9 %copy-start.18 = (s32[32]{0:T(128)}, s32[32]{0:T(128)S(1)}, u32[]{:S(2)}) copy-start(s32[32]{0:T(128)S(1)} %multiply_add_fusion.1) | copy-start | bytes 388
  9.0 18.3 %all-to-all-start = ((bf16[32,1,2]{2,1,0:T(2,128)(2,1)}), bf16[32,1,2]{2,1,0:T(2,128)(2,1)S(1)}, u32[]{:S(2)}, u32[]{:S(2)}) async-start(bf16[32,1,2]{2,1,0:T(2,128)(2,1)} %all_to_all.28), calls=%async_computation | async-start | bytes 32768 | tf_op jit(solution)/shard_map/all_to_all | solution.py:83
  27.4 20.2 %all-to-all-start.1 = ((bf16[32,2,4096]{2,1,0:T(2,128)(2,1)}), bf16[32,2,4096]{2,1,0:T(2,128)(2,1)S(1)}, u32[]{:S(2)}, u32[]{:S(2)}) async-start(bf16[32,2,4096]{2,1,0:T(2,128)(2,1)} %reshape.357), calls=%async_computation.1 | async-start | bytes 1048576 | tf_op jit(solution)/shard_map/all_to_all | solution.py:82
  32.1 17.8 %copy-start.20 = (f32[32]{0:T(128)}, f32[32]{0:T(128)S(1)}, u32[]{:S(2)}) copy-start(f32[32]{0:T(128)S(1)} %iota_convert_fusion) | copy-start | bytes 388
  47.8 9.8 %copy-start.9 = (bf16[256,128]{1,0:T(8,128)(2,1)S(1)}, bf16[256,128]{1,0:T(8,128)(2,1)}, u32[]{:S(2)}) copy-start(bf16[256,128]{1,0:T(8,128)(2,1)} %param.29) | copy-start | bytes 196612
  47.8 9.9 %copy-start.10 = (bf16[128,256]{1,0:T(8,128)(2,1)S(1)}, bf16[128,256]{1,0:T(8,128)(2,1)}, u32[]{:S(2)}) copy-start(bf16[128,256]{1,0:T(8,128)(2,1)} %param.26) | copy-start | bytes 196612
  47.8 9.9 %copy-start.11 = (bf16[128,256]{1,0:T(8,128)(2,1)S(1)}, bf16[128,256]{1,0:T(8,128)(2,1)}, u32[]{:S(2)}) copy-start(bf16[128,256]{1,0:T(8,128)(2,1)} %param.27) | copy-start | bytes 196612
  48.1 9.7 %copy-start.12 = (bf16[128,256]{1,0:T(8,128)(2,1)S(1)}, bf16[128,256]{1,0:T(8,128)(2,1)}, u32[]{:S(2)}) copy-start(bf16[128,256]{1,0:T(8,128)(2,1)} %param.28) | copy-start | bytes 196612
  48.1 9.7 %copy-start.7 = (bf16[128,1024]{1,0:T(8,128)(2,1)S(1)}, bf16[128,1024]{1,0:T(8,128)(2,1)}, u32[]{:S(2)}) copy-start(bf16[128,1024]{1,0:T(8,128)(2,1)} %param.34) | copy-start | bytes 786436
  49.9 32.3 %all-to-all-start.2 = ((bf16[8,256,512]{1,2,0:T(8,128)(2,1)}), bf16[8,256,512]{1,2,0:T(8,128)(2,1)}, u32[]{:S(2)}, u32[]{:S(2)}) async-start(bf16[8,256,512]{1,2,0:T(8,128)(2,1)} %broadcast_in_dim.15), calls=%async_computation.2 | async-start | bytes 4194304 | tf_op jit(solution)/shard_map/all_to_all | solution.py:98
  88.2 391.7 %all-to-all-start.3 = ((bf16[32,128,2048]{2,1,0:T(8,128)(2,1)}), bf16[32,128,2048]{2,1,0:T(8,128)(2,1)}, u32[]{:S(2)}, u32[]{:S(2)}) async-start(bf16[32,128,2048]{2,1,0:T(8,128)(2,1)} %stack.20), calls=%async_computation.3 | async-start | bytes 33554432 | tf_op jit(solution)/shard_map/all_to_all | solution.py:17
  484.2 18.2 %copy-start.16 = (s32[256]{0:T(256)S(1)}, s32[256]{0:T(256)}, u32[]{:S(2)}) copy-start(s32[256]{0:T(256)} %param.22) | copy-start | bytes 3076
  484.2 18.4 %copy-start.22 = (s32[256]{0:T(256)S(1)}, s32[256]{0:T(256)}, u32[]{:S(2)}) copy-start(s32[256]{0:T(256)} %param.23) | copy-start | bytes 3076
  484.2 207.8 %all-to-all-start.4 = ((bf16[32,1024,128]{1,2,0:T(8,128)(2,1)}), bf16[32,1024,128]{1,2,0:T(8,128)(2,1)}, u32[]{:S(2)}, u32[]{:S(2)}) async-start(bf16[32,1024,128]{1,2,0:T(8,128)(2,1)} %broadcast_in_dim.19), calls=%async_computation.4 | async-start | bytes 16777216 | tf_op jit(solution)/shard_map/all_to_all | solution.py:130
  501.8 6.1 copy-start.13
  501.8 6.1 copy-start.14
  501.8 264.6 %reduce-scatter.2.cloned.1.call-start = ((), (), s32[]{:S(2)}) async-start(), calls=%async_computation.7 | async-start | bytes 4718592 | tf_op jit(solution)/shard_map/reduce_scatter | solution.py:162
  503.3 7.2 copy-start.3
  548.7 9.8 %copy-start.6 = (bf16[1024,256]{1,0:T(8,128)(2,1)S(1)}, bf16[1024,256]{1,0:T(8,128)(2,1)}, u32[]{:S(2)}) copy-start(bf16[1024,256]{1,0:T(8,128)(2,1)} %param.31) | copy-start | bytes 1572868
  557.3 134.7 %copy-start.15 = (f32[1024]{0:T(1024)S(1)}, f32[1024]{0:T(1024)}, u32[]{:S(2)}) copy-start(f32[1024]{0:T(1024)} %param.35) | copy-start | bytes 12292
  706.7 59.8 %copy-start.17 = (f32[512]{0:T(512)S(1)}, f32[512]{0:T(512)}, u32[]{:S(2)}) copy-start(f32[512]{0:T(512)} %param.39) | copy-start | bytes 6148
  706.7 61.0 %copy-start.21 = (f32[32]{0:T(128)S(1)}, f32[32]{0:T(128)}, u32[]{:S(2)}) copy-start(f32[32]{0:T(128)} %copy-done.20) | copy-start | bytes 388
  706.7 90.0 %copy-start.19 = (s32[32]{0:T(128)S(1)}, s32[32]{0:T(128)}, u32[]{:S(2)}) copy-start(s32[32]{0:T(128)} %copy-done.18) | copy-start | bytes 388
  (5 other events, 17.8 us)
Sparse Core Ops, SparseCore 0:
  706.8 59.5 reduce-scatter.1
